TPU v7x, 256 devices: a whole 4x4x8 slice. The times are simulated.
256 devices in a mesh: row: 16 (over z_lo, y), col: 8 (over x, core), layer: 2 (over z_hi).
Axes of the slice: x: 4, y: 4, z: 8 (z_hi: 2, z_lo: 4; z = z_hi * 4 + z_lo), core: 2. Of those that a mesh axis runs over, the one named last changes fastest.
Arguments:
- density: float32 [2, 8192, 2048], P('layer', 'row', 'col'), may hold values from -6 to 6
- dens_mask: int32 [2, 128, 32], P('layer', 'row', 'col'), may hold values from 0 to 1, as said below
- hamiltonian: float32 [2, 2048, 16384], P('layer', 'row', 'col'), may hold values from -0.375 to 0.375
- ham_mask: int32 [2, 32, 256], P('layer', None, 'col'), may hold values from 0 to 1, as said below
- filter_mask: int32 [128, 256], P('row', 'col'), may hold values from 0 to 1, as said below
Outputs:
- product: float32 [8192, 16384], P('row', ('col', 'layer'))
Inputs may be any that keep to these rules, and one draw needn't show every extreme that they name: `dens_mask`: 1 where a density block is nonzero, else 0. `ham_mask`: 1 where a Hamiltonian block is nonzero, else 0. `filter_mask`: 1 where a result block is kept, else 0.
All inputs are finite; a program needn't handle non-finite values.
Results may differ from a plain program's by a relative error of at most 0.0001.
Values sent between devices are 32-bit elements; how exact they have to be, the bound alone decides.
No kernel may reach another device: no remote copies, remote signals or barrier semaphores. Data moves between devices by JAX's collectives and lax.ppermute only.
A program may use at most 128 MiB of HBM per device.

v0:
```python
import jax
import jax.numpy as jnp
from jax import lax
from jax.sharding import Mesh
from jax.sharding import PartitionSpec as P

BLOCK = 64
AXES = ("zl", "yh", "yl", "x", "core", "layer")
ROW = ("zl", "yh", "yl")
COL = ("x", "core")


def expand(block_mask):
    widened = jnp.repeat(block_mask.astype(jnp.float32), BLOCK, axis=-2)
    return jnp.repeat(widened, BLOCK, axis=-1)


def product_dot(a, b):
    return jnp.dot(a, b, precision=lax.Precision.HIGH, preferred_element_type=jnp.float32)


def gather_cols(block, index, n):
    parts = [block]
    for shift in range(1, n):
        parts.append(lax.ppermute(block, COL, [((i + shift) % n, i) for i in range(n)]))
    twice = jnp.concatenate(parts + parts, axis=1)
    return lax.dynamic_slice_in_dim(twice, (n - index) * block.shape[1], n * block.shape[1], axis=1)


def shards(density, dens_mask, hamiltonian, ham_mask, filter_mask, n_col):
    yl = lax.axis_index("yl")
    core = lax.axis_index("core")
    layer = lax.axis_index("layer")
    row = (lax.axis_index("zl") * 2 + lax.axis_index("yh")) * 2 + yl
    col = lax.axis_index("x") * 2 + core
    dens_vals = (density * expand(dens_mask))[0]
    ham_count = hamiltonian.shape[1]
    picked = lax.dynamic_slice_in_dim(
        ham_mask[0], row * (ham_count // BLOCK), ham_count // BLOCK, axis=0
    )
    ham_vals = hamiltonian[0] * expand(picked)
    half = ham_vals.shape[1] // 2
    kept = lax.dynamic_slice_in_dim(expand(filter_mask), layer * half, half, axis=1)
    pieces = {}
    for h in (0, 1):
        part = ham_vals[:, h * half : (h + 1) * half]
        for j in (0, 1):
            pieces[h, j] = lax.ppermute(
                part, ("yl", "core"), [(j * 2 + c, c * 2 + h) for c in (0, 1)]
            )
    contrib = jnp.where(
        core == 0,
        jnp.concatenate([pieces[0, 0], pieces[0, 1]], axis=0),
        jnp.concatenate([pieces[1, 0], pieces[1, 1]], axis=0),
    )
    ham_own = lax.all_gather(contrib, ("zl", "yh"), axis=0, tiled=True)
    ham_other = lax.ppermute(ham_own, "core", [(0, 1), (1, 0)])
    dens_own = gather_cols(dens_vals, col, n_col)
    dens_nbr = lax.ppermute(dens_own, ("yl", "core"), [(0, 2), (3, 1)])
    dens_rows = jnp.where(core == yl, dens_own, dens_nbr)
    part_own = product_dot(dens_rows, ham_own)
    part_other = product_dot(dens_rows, ham_other)

    def route(value, target_layer):
        perm = []
        for j in (0, 1):
            for k in (0, 1):
                for src in (0, 1):
                    perm.append((j * 4 + k * 2 + src, k * 4 + j * 2 + target_layer(k)))
        return [
            lax.ppermute(value, ("yl", "core", "layer"), [p for p in perm if p[0] % 2 == src])
            for src in (0, 1)
        ]

    got = route(part_own, lambda k: k) + route(part_other, lambda k: 1 - k)
    total = got[0] + got[1] + (got[2] + got[3])
    return total * kept


def solution(mesh):
    rows, cols, layers = mesh.devices.shape
    fine = Mesh(mesh.devices.reshape(rows // 4, 2, 2, cols // 2, 2, layers), AXES)
    return jax.shard_map(
        lambda *args: shards(*args, cols),
        mesh=fine,
        in_specs=(
            P("layer", ROW, COL),
            P("layer", ROW, COL),
            P("layer", ROW, COL),
            P("layer", None, COL),
            P(ROW, COL),
        ),
        out_specs=P(ROW, ("x", "core", "layer")),
        check_vma=False,
    )
```

profile of v0, /device:TPU:104, one launch (start us, length us, event | category | flops | bytes accessed | tf_op | source)
XLA Modules:
  0.0 483.6 jit_solution(13155475771516272750)
XLA Ops:
  7.6 1.6 copy.8
  10.0 4.3 collective-permute-start.11
  14.3 1.3 collective-permute-start.8
  15.6 1.9 collective-permute-start.9
  17.6 3.4 collective-permute-done.11
  21.0 3.9 collective-permute-done.8
  24.8 1.8 collective-permute-done.9
  26.6 2.1 maximum_select_fusion
  28.7 177.7 %all-gather.2.cloned.1.call-done = f32[2048,1024]{0,1:T(8,128)} async-done(((f32[256,1024]{0,1:T(8,128)}), f32[2048,1024]{0,1:T(8,128)}) %all-gather.2.cloned.1.call-update) | async-done | bytes 8388624 | tf_op jit(solution)/shard_map/all_gather | solution.py:56
  206.8 1.0 constant_dynamic-update-slice_fusion.15
  207.8 2.8 collective-permute-start
  211.5 2.4 collective-permute-start.3
  213.9 9.1 %collective-permute-done = f32[512,256]{0,1:T(8,128)S(1)} collective-permute-done((f32[512,256]{0,1:T(8,128)S(1)}, f32[512,256]{0,1:T(8,128)S(1)}, u32[]{:S(2)}, u32[]{:S(2)}) %collective-permute-start) | collective-permute-done | bytes 524320 | tf_op jit(solution)/shard_map/ppermute | solution.py:25
  222.9 1.0 collective-permute-start.4
  223.9 32.2 %collective-permute-done.1 = f32[512,256]{0,1:T(8,128)S(1)} collective-permute-done((f32[512,256]{0,1:T(8,128)S(1)}, f32[512,256]{0,1:T(8,128)S(1)}, u32[]{:S(2)}, u32[]{:S(2)}) %collective-permute-start.1) | collective-permute-done | bytes 524320 | tf_op jit(solution)/shard_map/ppermute | solution.py:25
  260.3 12.1 %collective-permute-done.5 = f32[512,256]{0,1:T(8,128)S(1)} collective-permute-done((f32[512,256]{0,1:T(8,128)S(1)}, f32[512,256]{0,1:T(8,128)S(1)}, u32[]{:S(2)}, u32[]{:S(2)}) %collective-permute-start.5) | collective-permute-done | bytes 524320 | tf_op jit(solution)/shard_map/ppermute | solution.py:25
  276.6 0.9 constant_dynamic-update-slice_fusion.4
  279.9 0.9 constant_dynamic-update-slice_fusion
  280.8 4.6 constant_dynamic-slice_fusion.1
  285.4 1.5 collective-permute-start.7
  286.9 49.2 %collective-permute-done.7 = f32[512,2048]{0,1:T(8,128)} collective-permute-done((f32[512,2048]{0,1:T(8,128)}, f32[512,2048]{0,1:T(8,128)}, u32[]{:S(2)}, u32[]{:S(2)}) %collective-permute-start.7) | collective-permute-done | bytes 4194336 | tf_op jit(solution)/shard_map/ppermute | solution.py:59
  336.1 17.9 %fusion.1 = f32[512,1024]{1,0:T(8,128)} fusion(f32[2048,1024]{0,1:T(8,128)} %all-gather.2.cloned.1.call-done, f32[512,2048]{0,1:T(8,128)} %constant_dynamic-slice_fusion.1, f32[512,2048]{0,1:T(8,128)} %collective-permute-done.7, pred[]{:T(512)S(6)} %eq.6), kind=kOutput, calls=%fused_computation.3 | convolution fusion | flops 6443499520 | bytes 18874368 | tf_op jit(solution)/shard_map/dot_general | solution.py:19
  354.0 2.8 collective-permute-start.12
  356.8 2.0 collective-permute-start.13
  358.8 17.9 %fusion = f32[512,1024]{1,0:T(8,128)} fusion(f32[2048,1024]{0,1:T(8,128)} %collective-permute-done.14, f32[512,2048]{0,1:T(8,128)} %constant_dynamic-slice_fusion.1, f32[512,2048]{0,1:T(8,128)} %collective-permute-done.7, pred[]{:T(512)S(6)} %eq.6), kind=kOutput, calls=%fused_computation.2 | convolution fusion | flops 6443499520 | bytes 18874368 | tf_op jit(solution)/shard_map/dot_general | solution.py:19
  376.7 3.6 collective-permute-start.15
  380.4 1.3 collective-permute-start.16
  382.7 1.8 copy.12
  384.5 4.3 collective-permute-done.12
  388.7 54.1 %collective-permute-done.15 = f32[512,1024]{1,0:T(8,128)} collective-permute-done((f32[512,1024]{1,0:T(8,128)}, f32[512,1024]{1,0:T(8,128)}, u32[]{:S(2)}, u32[]{:S(2)}) %collective-permute-start.15) | collective-permute-done | bytes 2097184 | tf_op jit(solution)/shard_map/ppermute | solution.py:71
  442.8 27.2 %collective-permute-done.16 = f32[512,1024]{1,0:T(8,128)} collective-permute-done((f32[512,1024]{1,0:T(8,128)}, f32[512,1024]{1,0:T(8,128)}, u32[]{:S(2)}, u32[]{:S(2)}) %collective-permute-start.16) | collective-permute-done | bytes 2097184 | tf_op jit(solution)/shard_map/ppermute | solution.py:71
  470.0 6.8 %add_multiply_fusion = f32[512,1024]{1,0:T(8,128)} fusion(f32[512,1024]{1,0:T(8,128)} %copy.12, f32[512,1024]{1,0:T(8,128)} %collective-permute-done.15, f32[512,1024]{1,0:T(8,128)} %collective-permute-done.16, f32[512,1024]{1,0:T(8,128)} %collective-permute-done.12, f32[512,1024]{1,0:T(8,128)} %collective-permute-done.13), kind=kLoop, calls=%fused_computation | loop fusion | flops 2097152 | bytes 12582912 | tf_op jit(solution)/shard_map/mul | solution.py:77
  (50 shorter events, 14.9 us)
Async XLA Ops:
  6.5 199.9 %copy-start = (f32[1,512,256]{2,1,0:T(8,128)S(1)}, f32[1,512,256]{2,1,0:T(8,128)}, u32[]{:S(2)}) copy-start(f32[1,512,256]{2,1,0:T(8,128)} %param.5) | copy-start | bytes 1572868
  6.5 200.1 %copy-start.2 = (s32[1,8,4]{1,2,0:T(4,128)S(1)}, s32[1,8,4]{1,2,0:T(4,128)}, u32[]{:S(2)}) copy-start(s32[1,8,4]{1,2,0:T(4,128)} %param.6) | copy-start | bytes 388
  6.5 199.9 %all-gather.2.cloned.1.call-start = ((), (), s32[]{:S(2)}) async-start(), calls=%async_computation | async-start | bytes 9437184 | tf_op jit(solution)/shard_map/all_gather | solution.py:56
  9.3 8.3 %collective-permute-start.10 = (f32[128,1024]{0,1:T(8,128)S(1)}, f32[128,1024]{0,1:T(8,128)S(1)}, u32[]{:S(2)}, u32[]{:S(2)}) collective-permute-start(f32[128,1024]{0,1:T(8,128)S(1)} %get-tuple-element.5), channel_id=1, source_target_pairs={{0,2},{2,18},{1,3},{3,19},{4,6},{6,22},{5,7},{7,23},{8,10},{10,26}... | collective-permute-start | bytes 1572872 | tf_op jit(solution)/shard_map/ppermute | solution.py:48
  10.0 11.0 %collective-permute-start.11 = (f32[128,1024]{0,1:T(8,128)S(1)}, f32[128,1024]{0,1:T(8,128)S(1)}, u32[]{:S(2)}, u32[]{:S(2)}) collective-permute-start(f32[128,1024]{0,1:T(8,128)S(1)} %get-tuple-element.5), channel_id=1, source_target_pairs={{16,2},{18,18},{17,3},{19,19},{20,6},{22,22},{21,7},{23,23},{24,10... | collective-permute-start | bytes 1572872 | tf_op jit(solution)/shard_map/ppermute | solution.py:48
  14.3 10.5 %collective-permute-start.8 = (f32[128,1024]{0,1:T(8,128)S(1)}, f32[128,1024]{0,1:T(8,128)S(1)}, u32[]{:S(2)}, u32[]{:S(2)}) collective-permute-start(f32[128,1024]{0,1:T(8,128)S(1)} %get-tuple-element.6), channel_id=1, source_target_pairs={{0,0},{2,16},{1,1},{3,17},{4,4},{6,20},{5,5},{7,21},{8,8},{10,24},... | collective-permute-start | bytes 1572872 | tf_op jit(solution)/shard_map/ppermute | solution.py:48
  15.6 11.0 %collective-permute-start.9 = (f32[128,1024]{0,1:T(8,128)S(1)}, f32[128,1024]{0,1:T(8,128)}, u32[]{:S(2)}, u32[]{:S(2)}) collective-permute-start(f32[128,1024]{0,1:T(8,128)S(1)} %get-tuple-element.6), channel_id=1, source_target_pairs={{16,0},{18,16},{17,1},{19,17},{20,4},{22,20},{21,5},{23,21},{24,8}... | collective-permute-start | bytes 1572872 | tf_op jit(solution)/shard_map/ppermute | solution.py:48
  206.5 152.4 %collective-permute-start.14 = (f32[2048,1024]{0,1:T(8,128)}, f32[2048,1024]{0,1:T(8,128)}, u32[]{:S(2)}, u32[]{:S(2)}) collective-permute-start(f32[2048,1024]{0,1:T(8,128)} %all-gather.2.cloned.1.call-done), channel_id=1, source_target_pairs={{0,2},{2,0},{1,3},{3,1},{4,6},{6,4},{5,7},{7,5},{8,10},{10,8},{9,1... | collective-permute-start | bytes 25165832 | tf_op jit(solution)/shard_map/ppermute | solution.py:57
  207.8 15.1 %collective-permute-start = (f32[512,256]{0,1:T(8,128)S(1)}, f32[512,256]{0,1:T(8,128)S(1)}, u32[]{:S(2)}, u32[]{:S(2)}) collective-permute-start(f32[512,256]{0,1:T(8,128)S(1)} %bitcast.23), channel_id=1, source_target_pairs={{2,0},{4,2},{6,4},{8,6},{10,8},{12,10},{14,12},{0,14},{3,1},{5,3},... | collective-permute-start | bytes 1572872 | tf_op jit(solution)/shard_map/ppermute | solution.py:25
  210.6 45.5 %collective-permute-start.1 = (f32[512,256]{0,1:T(8,128)S(1)}, f32[512,256]{0,1:T(8,128)S(1)}, u32[]{:S(2)}, u32[]{:S(2)}) collective-permute-start(f32[512,256]{0,1:T(8,128)S(1)} %bitcast.24), channel_id=1, source_target_pairs={{4,0},{6,2},{8,4},{10,6},{12,8},{14,10},{0,12},{2,14},{5,1},{7,3},... | collective-permute-start | bytes 1572872 | tf_op jit(solution)/shard_map/ppermute | solution.py:25
  211.5 45.5 %collective-permute-start.2 = (f32[512,256]{0,1:T(8,128)S(1)}, f32[512,256]{0,1:T(8,128)S(1)}, u32[]{:S(2)}, u32[]{:S(2)}) collective-permute-start(f32[512,256]{0,1:T(8,128)S(1)} %bitcast.25), channel_id=1, source_target_pairs={{6,0},{8,2},{10,4},{12,6},{14,8},{0,10},{2,12},{4,14},{7,1},{9,3},... | collective-permute-start | bytes 1572872 | tf_op jit(solution)/shard_map/ppermute | solution.py:25
  211.5 47.1 %collective-permute-start.3 = (f32[512,256]{0,1:T(8,128)S(1)}, f32[512,256]{0,1:T(8,128)S(1)}, u32[]{:S(2)}, u32[]{:S(2)}) collective-permute-start(f32[512,256]{0,1:T(8,128)S(1)} %bitcast.26), channel_id=1, source_target_pairs={{8,0},{10,2},{12,4},{14,6},{0,8},{2,10},{4,12},{6,14},{9,1},{11,3}... | collective-permute-start | bytes 1572872 | tf_op jit(solution)/shard_map/ppermute | solution.py:25
  222.9 36.5 %collective-permute-start.4 = (f32[512,256]{0,1:T(8,128)S(1)}, f32[512,256]{0,1:T(8,128)S(1)}, u32[]{:S(2)}, u32[]{:S(2)}) collective-permute-start(f32[512,256]{0,1:T(8,128)S(1)} %bitcast.27), channel_id=1, source_target_pairs={{10,0},{12,2},{14,4},{0,6},{2,8},{4,10},{6,12},{8,14},{11,1},{13,3... | collective-permute-start | bytes 1572872 | tf_op jit(solution)/shard_map/ppermute | solution.py:25
  256.1 16.3 %collective-permute-start.5 = (f32[512,256]{0,1:T(8,128)S(1)}, f32[512,256]{0,1:T(8,128)S(1)}, u32[]{:S(2)}, u32[]{:S(2)}) collective-permute-start(f32[512,256]{0,1:T(8,128)S(1)} %bitcast.28), channel_id=1, source_target_pairs={{12,0},{14,2},{0,4},{2,6},{4,8},{6,10},{8,12},{10,14},{13,1},{15,3... | collective-permute-start | bytes 1572872 | tf_op jit(solution)/shard_map/ppermute | solution.py:25
  256.9 16.3 %collective-permute-start.6 = (f32[512,256]{0,1:T(8,128)S(1)}, f32[512,256]{0,1:T(8,128)S(1)}, u32[]{:S(2)}, u32[]{:S(2)}) collective-permute-start(f32[512,256]{0,1:T(8,128)S(1)} %bitcast.29), channel_id=1, source_target_pairs={{14,0},{0,2},{2,4},{4,6},{6,8},{8,10},{10,12},{12,14},{15,1},{1,3}... | collective-permute-start | bytes 1572872 | tf_op jit(solution)/shard_map/ppermute | solution.py:25
  285.4 50.7 %collective-permute-start.7 = (f32[512,2048]{0,1:T(8,128)}, f32[512,2048]{0,1:T(8,128)}, u32[]{:S(2)}, u32[]{:S(2)}) collective-permute-start(f32[512,2048]{0,1:T(8,128)} %constant_dynamic-slice_fusion.1), channel_id=1, source_target_pairs={{0,16},{18,2},{1,17},{19,3},{4,20},{22,6},{5,21},{23,7},{8,24},{26... | collective-permute-start | bytes 12582920 | tf_op jit(solution)/shard_map/ppermute | solution.py:59
  354.0 27.6 %copy-start.1 = (s32[8,32]{1,0:T(8,128)S(1)}, s32[8,32]{1,0:T(8,128)}, u32[]{:S(2)}) copy-start(s32[8,32]{1,0:T(8,128)} %param.9) | copy-start | bytes 3076
  354.0 34.7 %collective-permute-start.12 = (f32[512,1024]{1,0:T(8,128)}, f32[512,1024]{1,0:T(8,128)}, u32[]{:S(2)}, u32[]{:S(2)}) collective-permute-start(f32[512,1024]{1,0:T(8,128)} %fusion.1), channel_id=1, source_target_pairs={{0,0},{2,17},{16,2},{18,19},{4,4},{6,21},{20,6},{22,23},{8,8},{10,... | collective-permute-start | bytes 6291464 | tf_op jit(solution)/shard_map/ppermute | solution.py:71
  356.8 31.9 %collective-permute-start.13 = (f32[512,1024]{1,0:T(8,128)}, f32[512,1024]{1,0:T(8,128)}, u32[]{:S(2)}, u32[]{:S(2)}) collective-permute-start(f32[512,1024]{1,0:T(8,128)} %fusion.1), channel_id=1, source_target_pairs={{1,0},{3,17},{17,2},{19,19},{5,4},{7,21},{21,6},{23,23},{9,8},{11,... | collective-permute-start | bytes 6291464 | tf_op jit(solution)/shard_map/ppermute | solution.py:71
  376.7 66.0 %collective-permute-start.15 = (f32[512,1024]{1,0:T(8,128)}, f32[512,1024]{1,0:T(8,128)}, u32[]{:S(2)}, u32[]{:S(2)}) collective-permute-start(f32[512,1024]{1,0:T(8,128)} %fusion), channel_id=1, source_target_pairs={{0,1},{2,16},{16,3},{18,18},{4,5},{6,20},{20,7},{22,22},{8,9},{10,... | collective-permute-start | bytes 6291464 | tf_op jit(solution)/shard_map/ppermute | solution.py:71
  380.4 89.6 %collective-permute-start.16 = (f32[512,1024]{1,0:T(8,128)}, f32[512,1024]{1,0:T(8,128)}, u32[]{:S(2)}, u32[]{:S(2)}) collective-permute-start(f32[512,1024]{1,0:T(8,128)} %fusion), channel_id=1, source_target_pairs={{1,1},{3,16},{17,3},{19,18},{5,5},{7,20},{21,7},{23,22},{9,9},{11,... | collective-permute-start | bytes 6291464 | tf_op jit(solution)/shard_map/ppermute | solution.py:71
Sparse Core Ops, SparseCore 0:
  28.9 177.5 all-gather.1
where the time goes:
time: 485 us; the launch traced here: 484 us
  waiting for transfers between devices  375 us (77%)
  matrix products  35.8 us (7%)
  starting transfers between devices  26.4 us (5%)
  local copies, waits for them, and re-layouts  22.2 us (5%)
  between operations  13.6 us (3%)
  other arithmetic  10.7 us (2%)
    all_gather x1, waiting for transfers between devices, shards(): ham_own = lax.all_gather(contrib, ('zl', 'yh'), axis=0, tiled=True)  178 us
    ppermute x4, waiting for transfers between devices, route(): lax.ppermute(value, ('yl', 'core', 'layer'), [p for p in perm if p[0] % 2...  85.5 us
    ppermute x7, waiting for transfers between devices, gather_cols(): lax.ppermute(block, COL, [((i + shift) % n, i) for i in range(n)])  53.4 us
    ppermute x1, waiting for transfers between devices, shards(): dens_nbr = lax.ppermute(dens_own, ('yl', 'core'), [(0, 2), (3, 1)])  49.2 us
    dot_general x2, matrix products, product_dot(): jnp.dot(a, b, precision=lax.Precision.HIGH, preferred_element_type=jnp.fl...  35.8 us
    unnamed x23, local copies, waits for them, and re-layouts  15.3 us
  transfers between devices with their start and end apart: 18, of which 11 were waited for; matrix products, arithmetic and copies ran while one was open for 12% of the time, Pallas kernels for 0%

commit v1 on v0

--- a/solution.py
+++ b/solution.py
@@ -53,7 +53,10 @@
         jnp.concatenate([pieces[0, 0], pieces[0, 1]], axis=0),
         jnp.concatenate([pieces[1, 0], pieces[1, 1]], axis=0),
     )
-    ham_own = lax.all_gather(contrib, ("zl", "yh"), axis=0, tiled=True)
+    ham_own = jnp.concatenate(
+        lax.all_to_all(jnp.stack([contrib] * lax.axis_size(("zl", "yh"))), ("zl", "yh"), 0, 0),
+        axis=0,
+    )
     ham_other = lax.ppermute(ham_own, "core", [(0, 1), (1, 0)])
     dens_own = gather_cols(dens_vals, col, n_col)
     dens_nbr = lax.ppermute(dens_own, ("yl", "core"), [(0, 2), (3, 1)])

time: 485 us -> 475 us (0.979)
  blocking collectives: 0 us -> 183 us
  waiting for transfers between devices: 375 us -> 202 us
  between operations: 13.6 us -> 0.24 us
  matrix products: 35.8 us -> 23.3 us
    all_to_all x0 -> x1, blocking collectives: none -> 183 us  [shards(): lax.all_to_all(jnp.stack([contrib] * lax.axis_size(('zl', 'yh'))), ('zl',...]
    all_gather x1 -> x0, waiting for transfers between devices: 178 us -> none  [shards(): ham_own = lax.all_gather(contrib, ('zl', 'yh'), axis=0, tiled=True)]
    dot_general x2, matrix products: 35.8 us -> 23.3 us  [product_dot(): jnp.dot(a, b, precision=lax.Precision.HIGH, preferred_element_type=jnp.fl...]
  transfers between devices with their start and end apart: 18 -> 17, of which waited for: 11 -> 10; matrix products, arithmetic and copies ran while one was open for 12% -> 9% of each run, Pallas kernels for 0% -> 0%
where the time goes in v1:
time: 475 us; the launch traced here: 471 us
  waiting for transfers between devices  202 us (43%)
  blocking collectives  183 us (39%)
  starting transfers between devices  30.2 us (6%)
  local copies, waits for them, and re-layouts  23.5 us (5%)
  matrix products  23.3 us (5%)
  other arithmetic  9.69 us (2%)
    all_to_all x1, blocking collectives, shards(): lax.all_to_all(jnp.stack([contrib] * lax.axis_size(('zl', 'yh'))), ('zl',...  183 us
    ppermute x4, waiting for transfers between devices, route(): lax.ppermute(value, ('yl', 'core', 'layer'), [p for p in perm if p[0] % 2...  87.7 us
    ppermute x7, waiting for transfers between devices, gather_cols(): lax.ppermute(block, COL, [((i + shift) % n, i) for i in range(n)])  53.4 us
    ppermute x1, waiting for transfers between devices, shards(): dens_nbr = lax.ppermute(dens_own, ('yl', 'core'), [(0, 2), (3, 1)])  51.7 us
    dot_general x2, matrix products, product_dot(): jnp.dot(a, b, precision=lax.Precision.HIGH, preferred_element_type=jnp.fl...  23.3 us
    unnamed x23, local copies, waits for them, and re-layouts  15.2 us
    ppermute x4, starting transfers between devices, route(): lax.ppermute(value, ('yl', 'core', 'layer'), [p for p in perm if p[0] % 2...  13.6 us
  transfers between devices with their start and end apart: 17, of which 10 were waited for; matrix products, arithmetic and copies ran while one was open for 9% of the time, Pallas kernels for 0%

profile of v1, /device:TPU:104, one launch (start us, length us, event | category | flops | bytes accessed | tf_op | source)
XLA Modules:
  0.0 471.3 jit_solution(1720147452877106249)
XLA Ops:
  1.0 1.6 copy.8
  3.4 4.3 collective-permute-start.11
  7.7 1.3 collective-permute-start.8
  9.0 1.9 collective-permute-start.9
  11.0 3.4 collective-permute-done.11
  14.4 3.9 collective-permute-done.8
  18.2 1.8 collective-permute-done.9
  20.0 1.1 maximum_select_fusion
  21.5 1.1 stack.2
  22.6 182.6 %all_to_all.5 = f32[8,256,1024]{2,1,0:T(8,128)} all-to-all(f32[8,256,1024]{2,1,0:T(8,128)S(1)} %stack.2), channel_id=1, replica_groups=mesh['zl'=4,'yh'=2,'yl'=2,'x'=4,'core'=2,'layer'=2] {'zl','yh'}, dimensions={0} | all-to-all | bytes 16777216 | tf_op jit(solution)/shard_map/all_to_all | solution.py:57
  205.5 0.9 constant_dynamic-update-slice_fusion.15
  206.5 2.9 collective-permute-start
  210.2 2.4 collective-permute-start.3
  212.6 9.1 %collective-permute-done = f32[512,256]{0,1:T(8,128)S(1)} collective-permute-done((f32[512,256]{0,1:T(8,128)S(1)}, f32[512,256]{0,1:T(8,128)S(1)}, u32[]{:S(2)}, u32[]{:S(2)}) %collective-permute-start) | collective-permute-done | bytes 524320 | tf_op jit(solution)/shard_map/ppermute | solution.py:25
  221.7 0.9 collective-permute-start.4
  222.6 32.2 %collective-permute-done.1 = f32[512,256]{0,1:T(8,128)S(1)} collective-permute-done((f32[512,256]{0,1:T(8,128)S(1)}, f32[512,256]{0,1:T(8,128)S(1)}, u32[]{:S(2)}, u32[]{:S(2)}) %collective-permute-start.1) | collective-permute-done | bytes 524320 | tf_op jit(solution)/shard_map/ppermute | solution.py:25
  259.0 12.1 %collective-permute-done.5 = f32[512,256]{0,1:T(8,128)S(1)} collective-permute-done((f32[512,256]{0,1:T(8,128)S(1)}, f32[512,256]{0,1:T(8,128)S(1)}, u32[]{:S(2)}, u32[]{:S(2)}) %collective-permute-start.5) | collective-permute-done | bytes 524320 | tf_op jit(solution)/shard_map/ppermute | solution.py:25
  278.6 0.9 constant_dynamic-update-slice_fusion
  279.5 4.6 constant_dynamic-slice_fusion.1
  284.1 1.3 collective-permute-start.7
  285.4 51.7 %collective-permute-done.7 = f32[512,2048]{0,1:T(8,128)} collective-permute-done((f32[512,2048]{0,1:T(8,128)}, f32[512,2048]{0,1:T(8,128)}, u32[]{:S(2)}, u32[]{:S(2)}) %collective-permute-start.7) | collective-permute-done | bytes 4194336 | tf_op jit(solution)/shard_map/ppermute | solution.py:62
  337.1 11.6 %fusion.1 = f32[512,1024]{1,0:T(8,128)} fusion(f32[2048,1024]{1,0:T(8,128)} %bitcast.6, f32[512,2048]{0,1:T(8,128)} %constant_dynamic-slice_fusion.1, f32[512,2048]{0,1:T(8,128)} %collective-permute-done.7, pred[]{:T(512)S(6)} %eq.6), kind=kOutput, calls=%fused_computation.3 | convolution fusion | flops 6443499520 | bytes 18874368 | tf_op jit(solution)/shard_map/dot_general | solution.py:19
  348.7 2.8 collective-permute-start.12
  351.5 2.0 collective-permute-start.13
  353.5 11.7 %fusion = f32[512,1024]{1,0:T(8,128)} fusion(f32[2048,1024]{1,0:T(8,128)} %collective-permute-done.14, f32[512,2048]{0,1:T(8,128)} %constant_dynamic-slice_fusion.1, f32[512,2048]{0,1:T(8,128)} %collective-permute-done.7, pred[]{:T(512)S(6)} %eq.6), kind=kOutput, calls=%fused_computation.2 | convolution fusion | flops 6443499520 | bytes 18874368 | tf_op jit(solution)/shard_map/dot_general | solution.py:19
  365.2 7.5 %collective-permute-start.15 = (f32[512,1024]{1,0:T(8,128)}, f32[512,1024]{1,0:T(8,128)}, u32[]{:S(2)}, u32[]{:S(2)}) collective-permute-start(f32[512,1024]{1,0:T(8,128)} %fusion), channel_id=1, source_target_pairs={{0,1},{2,16},{16,3},{18,18},{4,5},{6,20},{20,7},{22,22},{8,9},{10,... | collective-permute-start | bytes 6291464 | tf_op jit(solution)/shard_map/ppermute | solution.py:74
  372.7 1.3 collective-permute-start.16
  375.0 1.8 copy.13
  376.8 10.4 %collective-permute-done.12 = f32[512,1024]{1,0:T(8,128)} collective-permute-done((f32[512,1024]{1,0:T(8,128)}, f32[512,1024]{1,0:T(8,128)}, u32[]{:S(2)}, u32[]{:S(2)}) %collective-permute-start.12) | collective-permute-done | bytes 2097184 | tf_op jit(solution)/shard_map/ppermute | solution.py:74
  387.2 54.2 %collective-permute-done.15 = f32[512,1024]{1,0:T(8,128)} collective-permute-done((f32[512,1024]{1,0:T(8,128)}, f32[512,1024]{1,0:T(8,128)}, u32[]{:S(2)}, u32[]{:S(2)}) %collective-permute-start.15) | collective-permute-done | bytes 2097184 | tf_op jit(solution)/shard_map/ppermute | solution.py:74
  441.3 23.1 %collective-permute-done.16 = f32[512,1024]{1,0:T(8,128)} collective-permute-done((f32[512,1024]{1,0:T(8,128)}, f32[512,1024]{1,0:T(8,128)}, u32[]{:S(2)}, u32[]{:S(2)}) %collective-permute-start.16) | collective-permute-done | bytes 2097184 | tf_op jit(solution)/shard_map/ppermute | solution.py:74
  464.4 6.8 %add_multiply_fusion = f32[512,1024]{1,0:T(8,128)} fusion(f32[512,1024]{1,0:T(8,128)} %copy.13, f32[512,1024]{1,0:T(8,128)} %collective-permute-done.15, f32[512,1024]{1,0:T(8,128)} %collective-permute-done.16, f32[512,1024]{1,0:T(8,128)} %collective-permute-done.12, f32[512,1024]{1,0:T(8,128)} %collective-permute-done.13), kind=kLoop, calls=%fused_computation | loop fusion | flops 2097152 | bytes 12582912 | tf_op jit(solution)/shard_map/mul | solution.py:80
  (50 shorter events, 16.0 us)
Async XLA Ops:
  2.7 8.3 %collective-permute-start.10 = (f32[128,1024]{0,1:T(8,128)S(1)}, f32[128,1024]{0,1:T(8,128)S(1)}, u32[]{:S(2)}, u32[]{:S(2)}) collective-permute-start(f32[128,1024]{0,1:T(8,128)S(1)} %get-tuple-element.5), channel_id=1, source_target_pairs={{0,2},{2,18},{1,3},{3,19},{4,6},{6,22},{5,7},{7,23},{8,10},{10,26}... | collective-permute-start | bytes 1572872 | tf_op jit(solution)/shard_map/ppermute | solution.py:48
  3.4 11.0 %collective-permute-start.11 = (f32[128,1024]{0,1:T(8,128)S(1)}, f32[128,1024]{0,1:T(8,128)S(1)}, u32[]{:S(2)}, u32[]{:S(2)}) collective-permute-start(f32[128,1024]{0,1:T(8,128)S(1)} %get-tuple-element.5), channel_id=1, source_target_pairs={{16,2},{18,18},{17,3},{19,19},{20,6},{22,22},{21,7},{23,23},{24,10... | collective-permute-start | bytes 1572872 | tf_op jit(solution)/shard_map/ppermute | solution.py:48
  7.7 10.5 %collective-permute-start.8 = (f32[128,1024]{0,1:T(8,128)S(1)}, f32[128,1024]{0,1:T(8,128)S(1)}, u32[]{:S(2)}, u32[]{:S(2)}) collective-permute-start(f32[128,1024]{0,1:T(8,128)S(1)} %get-tuple-element.6), channel_id=1, source_target_pairs={{0,0},{2,16},{1,1},{3,17},{4,4},{6,20},{5,5},{7,21},{8,8},{10,24},... | collective-permute-start | bytes 1572872 | tf_op jit(solution)/shard_map/ppermute | solution.py:48
  9.0 11.0 %collective-permute-start.9 = (f32[128,1024]{0,1:T(8,128)S(1)}, f32[128,1024]{0,1:T(8,128)}, u32[]{:S(2)}, u32[]{:S(2)}) collective-permute-start(f32[128,1024]{0,1:T(8,128)S(1)} %get-tuple-element.6), channel_id=1, source_target_pairs={{16,0},{18,16},{17,1},{19,17},{20,4},{22,20},{21,5},{23,21},{24,8}... | collective-permute-start | bytes 1572872 | tf_op jit(solution)/shard_map/ppermute | solution.py:48
  22.5 182.6 %copy-start = (f32[1,512,256]{2,1,0:T(8,128)S(1)}, f32[1,512,256]{2,1,0:T(8,128)}, u32[]{:S(2)}) copy-start(f32[1,512,256]{2,1,0:T(8,128)} %param.5) | copy-start | bytes 1572868
  22.6 182.8 %copy-start.2 = (s32[1,8,4]{1,2,0:T(4,128)S(1)}, s32[1,8,4]{1,2,0:T(4,128)}, u32[]{:S(2)}) copy-start(s32[1,8,4]{1,2,0:T(4,128)} %param.6) | copy-start | bytes 388
  205.2 148.4 %collective-permute-start.14 = (f32[2048,1024]{1,0:T(8,128)}, f32[2048,1024]{1,0:T(8,128)}, u32[]{:S(2)}, u32[]{:S(2)}) collective-permute-start(f32[2048,1024]{1,0:T(8,128)} %bitcast.6), channel_id=1, source_target_pairs={{0,2},{2,0},{1,3},{3,1},{4,6},{6,4},{5,7},{7,5},{8,10},{10,8},{9,1... | collective-permute-start | bytes 25165832 | tf_op jit(solution)/shard_map/ppermute | solution.py:60
  206.5 15.2 %collective-permute-start = (f32[512,256]{0,1:T(8,128)S(1)}, f32[512,256]{0,1:T(8,128)S(1)}, u32[]{:S(2)}, u32[]{:S(2)}) collective-permute-start(f32[512,256]{0,1:T(8,128)S(1)} %bitcast.24), channel_id=1, source_target_pairs={{2,0},{4,2},{6,4},{8,6},{10,8},{12,10},{14,12},{0,14},{3,1},{5,3},... | collective-permute-start | bytes 1572872 | tf_op jit(solution)/shard_map/ppermute | solution.py:25
  209.4 45.5 %collective-permute-start.1 = (f32[512,256]{0,1:T(8,128)S(1)}, f32[512,256]{0,1:T(8,128)S(1)}, u32[]{:S(2)}, u32[]{:S(2)}) collective-permute-start(f32[512,256]{0,1:T(8,128)S(1)} %bitcast.25), channel_id=1, source_target_pairs={{4,0},{6,2},{8,4},{10,6},{12,8},{14,10},{0,12},{2,14},{5,1},{7,3},... | collective-permute-start | bytes 1572872 | tf_op jit(solution)/shard_map/ppermute | solution.py:25
  210.2 45.5 %collective-permute-start.2 = (f32[512,256]{0,1:T(8,128)S(1)}, f32[512,256]{0,1:T(8,128)S(1)}, u32[]{:S(2)}, u32[]{:S(2)}) collective-permute-start(f32[512,256]{0,1:T(8,128)S(1)} %bitcast.26), channel_id=1, source_target_pairs={{6,0},{8,2},{10,4},{12,6},{14,8},{0,10},{2,12},{4,14},{7,1},{9,3},... | collective-permute-start | bytes 1572872 | tf_op jit(solution)/shard_map/ppermute | solution.py:25
  210.2 47.2 %collective-permute-start.3 = (f32[512,256]{0,1:T(8,128)S(1)}, f32[512,256]{0,1:T(8,128)S(1)}, u32[]{:S(2)}, u32[]{:S(2)}) collective-permute-start(f32[512,256]{0,1:T(8,128)S(1)} %bitcast.27), channel_id=1, source_target_pairs={{8,0},{10,2},{12,4},{14,6},{0,8},{2,10},{4,12},{6,14},{9,1},{11,3}... | collective-permute-start | bytes 1572872 | tf_op jit(solution)/shard_map/ppermute | solution.py:25
  221.7 36.5 %collective-permute-start.4 = (f32[512,256]{0,1:T(8,128)S(1)}, f32[512,256]{0,1:T(8,128)S(1)}, u32[]{:S(2)}, u32[]{:S(2)}) collective-permute-start(f32[512,256]{0,1:T(8,128)S(1)} %bitcast.28), channel_id=1, source_target_pairs={{10,0},{12,2},{14,4},{0,6},{2,8},{4,10},{6,12},{8,14},{11,1},{13,3... | collective-permute-start | bytes 1572872 | tf_op jit(solution)/shard_map/ppermute | solution.py:25
  254.8 16.3 %collective-permute-start.5 = (f32[512,256]{0,1:T(8,128)S(1)}, f32[512,256]{0,1:T(8,128)S(1)}, u32[]{:S(2)}, u32[]{:S(2)}) collective-permute-start(f32[512,256]{0,1:T(8,128)S(1)} %bitcast.29), channel_id=1, source_target_pairs={{12,0},{14,2},{0,4},{2,6},{4,8},{6,10},{8,12},{10,14},{13,1},{15,3... | collective-permute-start | bytes 1572872 | tf_op jit(solution)/shard_map/ppermute | solution.py:25
  255.7 16.3 %collective-permute-start.6 = (f32[512,256]{0,1:T(8,128)S(1)}, f32[512,256]{0,1:T(8,128)S(1)}, u32[]{:S(2)}, u32[]{:S(2)}) collective-permute-start(f32[512,256]{0,1:T(8,128)S(1)} %bitcast.30), channel_id=1, source_target_pairs={{14,0},{0,2},{2,4},{4,6},{6,8},{8,10},{10,12},{12,14},{15,1},{1,3}... | collective-permute-start | bytes 1572872 | tf_op jit(solution)/shard_map/ppermute | solution.py:25
  284.1 53.0 %collective-permute-start.7 = (f32[512,2048]{0,1:T(8,128)}, f32[512,2048]{0,1:T(8,128)}, u32[]{:S(2)}, u32[]{:S(2)}) collective-permute-start(f32[512,2048]{0,1:T(8,128)} %constant_dynamic-slice_fusion.1), channel_id=1, source_target_pairs={{0,16},{18,2},{1,17},{19,3},{4,20},{22,6},{5,21},{23,7},{8,24},{26... | collective-permute-start | bytes 12582920 | tf_op jit(solution)/shard_map/ppermute | solution.py:62
  348.7 25.3 %copy-start.1 = (s32[8,32]{1,0:T(8,128)S(1)}, s32[8,32]{1,0:T(8,128)}, u32[]{:S(2)}) copy-start(s32[8,32]{1,0:T(8,128)} %param.9) | copy-start | bytes 3076
  348.7 38.4 %collective-permute-start.12 = (f32[512,1024]{1,0:T(8,128)}, f32[512,1024]{1,0:T(8,128)}, u32[]{:S(2)}, u32[]{:S(2)}) collective-permute-start(f32[512,1024]{1,0:T(8,128)} %fusion.1), channel_id=1, source_target_pairs={{0,0},{2,17},{16,2},{18,19},{4,4},{6,21},{20,6},{22,23},{8,8},{10,... | collective-permute-start | bytes 6291464 | tf_op jit(solution)/shard_map/ppermute | solution.py:74
  351.5 35.7 %collective-permute-start.13 = (f32[512,1024]{1,0:T(8,128)}, f32[512,1024]{1,0:T(8,128)}, u32[]{:S(2)}, u32[]{:S(2)}) collective-permute-start(f32[512,1024]{1,0:T(8,128)} %fusion.1), channel_id=1, source_target_pairs={{1,0},{3,17},{17,2},{19,19},{5,4},{7,21},{21,6},{23,23},{9,8},{11,... | collective-permute-start | bytes 6291464 | tf_op jit(solution)/shard_map/ppermute | solution.py:74
  365.2 76.2 %collective-permute-start.15 = (f32[512,1024]{1,0:T(8,128)}, f32[512,1024]{1,0:T(8,128)}, u32[]{:S(2)}, u32[]{:S(2)}) collective-permute-start(f32[512,1024]{1,0:T(8,128)} %fusion), channel_id=1, source_target_pairs={{0,1},{2,16},{16,3},{18,18},{4,5},{6,20},{20,7},{22,22},{8,9},{10,... | collective-permute-start | bytes 6291464 | tf_op jit(solution)/shard_map/ppermute | solution.py:74
  372.7 91.8 %collective-permute-start.16 = (f32[512,1024]{1,0:T(8,128)}, f32[512,1024]{1,0:T(8,128)}, u32[]{:S(2)}, u32[]{:S(2)}) collective-permute-start(f32[512,1024]{1,0:T(8,128)} %fusion), channel_id=1, source_target_pairs={{1,1},{3,16},{17,3},{19,18},{5,5},{7,20},{21,7},{23,22},{9,9},{11,... | collective-permute-start | bytes 6291464 | tf_op jit(solution)/shard_map/ppermute | solution.py:74
